TPU v7x, 256 devices: a whole 4x4x8 slice. The times are simulated.
256 devices in a mesh: dp: 16 (over y_lo, x, core), tensor: 16 (over y_hi, z).
Axes of the slice: x: 4, y: 4 (y_hi: 2, y_lo: 2; y = y_hi * 2 + y_lo), z: 8, core: 2. Of those that a mesh axis runs over, the one named last changes fastest.
Arguments:
- tokens: bfloat16 [12288, 8192], P(('dp', 'tensor')), may hold values from -6 to 6
- q_weight: bfloat16 [8192, 8192], P(None, 'tensor'), may hold values from -0.0625 to 0.0625
- pool_down: bfloat16 [128, 64, 8192], P('dp', None, 'tensor'), may hold values from -0.0625 to 0.0625
- pool_up: bfloat16 [128, 64, 8192], P('dp', None, 'tensor'), may hold values from -0.75 to 0.75
- block_units: int32 [16, 8], replicated, may hold values from 1 to 24, 48 in all within a row
- adapter_ids: int32 [16, 8], replicated, may hold values from 0 to 127, as said below
- location: int32 [128], replicated, may hold values from 0 to 127, as said below
Outputs:
- queries: bfloat16 [12288, 8192], P('dp', 'tensor')
Inputs may be any that keep to these rules, and one draw needn't show every extreme that they name: `adapter_ids`: the 8 adapters of one group lie in pool rows of 8 different dp shards (row location[a] lies on shard location[a] // 8). A permutation: adapter a is held in pool row location[a]. `block_units`: each group's blocks sum to 48; the largest is exactly 24.
All inputs are finite; a program needn't handle non-finite values.
Results may differ from a plain program's by a relative error of at most 0.0029.
Values may be sent and summed in bfloat16 or wider, within the bound.
No kernel may reach another device: no remote copies, remote signals or barrier semaphores. Data moves between devices by JAX's collectives and lax.ppermute only.
A program may use at most 128 MiB of HBM per device.

v0:
```python
import jax
import jax.numpy as jnp
from jax import lax
from jax.sharding import PartitionSpec as P

adapter_scale = 0.5


def tenant_mask(pool_unit_row, group_rows, tenants):
    block_ends = 16 * jnp.cumsum(pool_unit_row)
    positions = jnp.arange(group_rows, dtype=jnp.int32)
    tenant_index = jnp.sum((positions[:, None] >= block_ends[None, :]).astype(jnp.int32), axis=1)
    return tenant_index[:, None] == jnp.arange(tenants, dtype=jnp.int32)[None, :]


def on_device(tokens, q_weight, pool_down, pool_up, block_units, adapter_ids, location):
    my_group = lax.axis_index("dp")
    groups = adapter_ids.shape[0]
    tenants = adapter_ids.shape[1]
    pool_dev = pool_down.shape[0]
    rank_size = pool_down.shape[1]
    local_width = pool_down.shape[2]
    columns = q_weight.shape[1]
    slot_ids = jnp.take(location, adapter_ids, axis=0)
    slot_shard = slot_ids // pool_dev
    slot_row = slot_ids % pool_dev
    from_me = slot_shard == my_group
    send_row = jnp.sum(jnp.where(from_me, slot_row, 0), axis=1)
    both = jnp.concatenate([pool_down, pool_up], axis=1)
    send = jnp.take(both, send_row, axis=0)
    recv = lax.all_to_all(send, "dp", 0, 0, tiled=True)
    my_src = lax.dynamic_index_in_dim(slot_shard, my_group, 0, keepdims=False)
    panels = jnp.take(recv, my_src, axis=0)
    down_flat = panels[:, :rank_size, :].reshape(tenants * rank_size, local_width)
    up_flat = panels[:, rank_size:, :].reshape(tenants * rank_size, columns)
    width_start = lax.axis_index("tensor") * local_width
    row_block = lax.all_gather(tokens, "tensor", axis=0, tiled=True)
    base_projection = jnp.dot(row_block, q_weight, preferred_element_type=jnp.float32)
    local_cols = lax.dynamic_slice_in_dim(row_block, width_start, local_width, 1)
    wide_part = lax.dot_general(
        local_cols, down_flat, (((1,), (1,)), ((), ())), preferred_element_type=jnp.float32
    )
    group_rows = wide_part.shape[0]
    wide_part = wide_part.reshape(group_rows, tenants, rank_size)
    pool_unit_row = lax.dynamic_index_in_dim(block_units, my_group, 0, keepdims=False)
    tenant_masks = tenant_mask(pool_unit_row, group_rows, tenants)
    partial_low = jnp.sum(
        jnp.where(tenant_masks[:, :, None], wide_part, jnp.zeros((), jnp.float32)), axis=1
    )
    low_part = lax.psum_scatter(partial_low, "tensor", scatter_dimension=0, tiled=True)
    low_rank = lax.all_gather(low_part, "tensor", axis=0, tiled=True).astype(jnp.bfloat16)
    low_wide = jnp.where(
        tenant_masks[:, :, None], low_rank[:, None, :], jnp.zeros((), jnp.bfloat16)
    )
    adapter_contribution = jnp.dot(
        low_wide.reshape(group_rows, tenants * rank_size),
        up_flat,
        preferred_element_type=jnp.float32,
    )
    return (base_projection + adapter_scale * adapter_contribution).astype(jnp.bfloat16)


def solution(mesh):
    placed = (
        P(("dp", "tensor"), None),
        P(None, "tensor"),
        P("dp", None, "tensor"),
        P("dp", None, "tensor"),
        P(),
        P(),
        P(),
    )
    return jax.shard_map(
        on_device, mesh=mesh, in_specs=placed, out_specs=P("dp", "tensor"), check_vma=False
    )
```

profile of v0, /device:TPU:2, one launch (start us, length us, event | category | flops | bytes accessed | tf_op | source)
XLA Modules:
  0.0 472.1 jit_solution(14032850056442191799)
XLA Ops:
  6.5 0.0 copy-start
  6.5 0.0 all-gather.2.cloned.1.call-start
  6.5 0.7 all-gather.2.cloned.1.call-update
  7.3 0.8 copy.24
  8.0 0.1 reshape.115
  8.1 0.0 copy-done.1
  8.1 0.0 copy-start.2
  8.2 0.0 copy-start.3
  8.2 1.2 gather_fusion
  9.4 0.1 reshape.114
  9.5 0.1 add_select_fusion.1
  9.7 0.1 pad_maximum_fusion
  9.7 0.7 gather_fusion.1
  10.4 1.6 broadcast_select_fusion
  12.1 5.9 %all-to-all-start = ((bf16[16,128,512]{2,1,0:T(8,128)(2,1)}), bf16[16,128,512]{2,1,0:T(8,128)(2,1)S(1)}, u32[]{:S(2)}, u32[]{:S(2)}) async-start(bf16[16,128,512]{2,1,0:T(8,128)(2,1)} %broadcast_select_fusion), calls=%async_computation | async-start | bytes 4194304 | tf_op jit(solution)/shard_map/all_to_all | solution.py:31
  17.9 0.0 reduce-scatter.4.cloned.1.call-start
  18.0 0.0 copy-done
  18.0 0.2 dynamic-slice_reduce_fusion
  18.2 0.2 reduce-window.8
  18.4 0.1 convert_reduce_fusion
  18.5 28.0 %all-to-all-done = bf16[16,128,512]{2,1,0:T(8,128)(2,1)S(1)} async-done(((bf16[16,128,512]{2,1,0:T(8,128)(2,1)}), bf16[16,128,512]{2,1,0:T(8,128)(2,1)S(1)}, u32[]{:S(2)}, u32[]{:S(2)}) %all-to-all-start) | async-done | bytes 2097184 | tf_op jit(solution)/shard_map/all_to_all | solution.py:31
  46.5 0.6 gather_fusion.2
  47.1 0.2 broadcast_select_fusion.1
  47.3 160.2 %all-gather.2.cloned.1.call-done = bf16[768,8192]{1,0:T(8,128)(2,1)} async-done(((bf16[48,8192]{1,0:T(8,128)(2,1)}), bf16[768,8192]{1,0:T(8,128)(2,1)}) %all-gather.2.cloned.1.call-update) | async-done | bytes 12582928 | tf_op jit(solution)/shard_map/all_gather | solution.py:37
  207.5 1.8 select_reduce_fusion
  209.3 0.9 copy.29
  210.2 0.0 reduce-scatter.4.cloned.1.call-update
  210.2 201.0 %reduce-scatter.4.cloned.1.call-done = f32[48,64]{1,0:T(8,128)} async-done(((f32[768,64]{1,0:T(8,128)}), f32[48,64]{1,0:T(8,128)}) %reduce-scatter.4.cloned.1.call-update) | async-done | bytes 12304 | tf_op jit(solution)/shard_map/reduce_scatter | solution.py:50
  411.2 40.6 %all_gather.7 = f32[768,64]{1,0:T(8,128)S(1)} all-gather(f32[48,64]{1,0:T(8,128)} %reduce-scatter.4.cloned.1.call-done), channel_id=1, replica_groups=mesh['dp'=16,'tensor'=16] {'tensor'}, dimensions={0}, use_global_device_ids=true | all-gather | bytes 208896 | tf_op jit(solution)/shard_map/all_gather | solution.py:51
  451.8 0.1 copy.28
  451.9 0.6 fusion.3
  452.5 12.8 %fusion.1 = bf16[768,512]{1,0:T(8,128)(2,1)} fusion(f32[768,512,1]{1,0,2:T(8,128)S(1)} %fusion.3, bf16[768,8192]{1,0:T(8,128)(2,1)} %all-gather.2.cloned.1.call-done, bf16[8192,512]{1,0:T(8,128)(2,1)} %param.8), kind=kOutput, calls=%fused_computation.6 | convolution fusion | flops 6443630592 | bytes 23330816 | tf_op jit(solution)/shard_map/dot_general | solution.py:38
  (13 shorter events, 0.1 us)
Async XLA Ops:
  6.5 11.4 %copy-start = (s32[16,8]{0,1:T(8,128)S(1)}, s32[16,8]{0,1:T(8,128)}, u32[]{:S(2)}) copy-start(s32[16,8]{0,1:T(8,128)} %param.11) | copy-start | bytes 1540
  6.5 1.6 copy-start.1
  6.5 201.0 %all-gather.2.cloned.1.call-start = ((), (), s32[]{:S(2)}) async-start(), calls=%async_computation.2 | async-start | bytes 13369344 | tf_op jit(solution)/shard_map/all_gather | solution.py:37
  8.1 1.5 copy-start.2
  8.2 1.5 copy-start.3
  12.1 34.4 %all-to-all-start = ((bf16[16,128,512]{2,1,0:T(8,128)(2,1)}), bf16[16,128,512]{2,1,0:T(8,128)(2,1)S(1)}, u32[]{:S(2)}, u32[]{:S(2)}) async-start(bf16[16,128,512]{2,1,0:T(8,128)(2,1)} %broadcast_select_fusion), calls=%async_computation | async-start | bytes 4194304 | tf_op jit(solution)/shard_map/all_to_all | solution.py:31
  17.9 393.3 %reduce-scatter.4.cloned.1.call-start = ((), (), s32[]{:S(2)}) async-start(), calls=%async_computation.3 | async-start | bytes 417792 | tf_op jit(solution)/shard_map/reduce_scatter | solution.py:50
Sparse Core Ops, SparseCore 0:
  9.9 197.5 all-gather.1
  211.3 199.8 reduce-scatter.3
where the time goes:
time: 472 us
  waiting for transfers between devices  390 us (83%)
  blocking collectives  40.6 us (9%)
  matrix products  15.1 us (3%)
  between operations  13.6 us (3%)
  starting transfers between devices  5.9 us (1%)
    reduce_scatter x1, waiting for transfers between devices, on_device(): lax.psum_scatter(partial_low, 'tensor', scatter_dimension=0, tiled=True)  201 us
    all_gather x1, waiting for transfers between devices, on_device(): row_block = lax.all_gather(tokens, 'tensor', axis=0, tiled=True)  160 us
    all_gather x1, blocking collectives, on_device(): lax.all_gather(low_part, 'tensor', axis=0, tiled=True).astype(jnp.bfloat16)  40.6 us
    all_to_all x1, waiting for transfers between devices, on_device(): recv = lax.all_to_all(send, 'dp', 0, 0, tiled=True)  28 us
    dot_general x1, matrix products, on_device(): jnp.dot(row_block, q_weight, preferred_element_type=jnp.float32)  12.8 us
  transfers between devices with their start and end apart: 3, of which 3 were waited for; matrix products, arithmetic and copies ran while one was open for 1% of the time, Pallas kernels for 0%

commit v1 on v0

--- a/solution.py
+++ b/solution.py
@@ -34,7 +34,9 @@
     down_flat = panels[:, :rank_size, :].reshape(tenants * rank_size, local_width)
     up_flat = panels[:, rank_size:, :].reshape(tenants * rank_size, columns)
     width_start = lax.axis_index("tensor") * local_width
-    row_block = lax.all_gather(tokens, "tensor", axis=0, tiled=True)
+    row_block = jnp.concatenate(
+        lax.all_to_all(jnp.stack([tokens] * lax.axis_size("tensor")), "tensor", 0, 0), axis=0
+    )
     base_projection = jnp.dot(row_block, q_weight, preferred_element_type=jnp.float32)
     local_cols = lax.dynamic_slice_in_dim(row_block, width_start, local_width, 1)
     wide_part = lax.dot_general(

time: 472 us -> 614 us (1.30)
  waiting for transfers between devices: 390 us -> 491 us
  blocking collectives: 40.6 us -> 70.7 us
    all_to_all x1, waiting for transfers between devices: 28 us -> 279 us  [on_device(): lax.all_to_all(jnp.stack([tokens] * lax.axis_size('tensor')), 'tensor', 0...]
    all_gather x1 -> x0, waiting for transfers between devices: 160 us -> none  [on_device(): row_block = lax.all_gather(tokens, 'tensor', axis=0, tiled=True)]
    all_to_all x0 -> x1, blocking collectives: none -> 30.2 us  [on_device(): recv = lax.all_to_all(send, 'dp', 0, 0, tiled=True)]
    reduce_scatter x1, waiting for transfers between devices: 201 us -> 213 us  [on_device(): lax.psum_scatter(partial_low, 'tensor', scatter_dimension=0, tiled=True)]
  transfers between devices with their start and end apart: 3 -> 2, of which waited for: 3 -> 2; matrix products, arithmetic and copies ran while one was open for 1% -> 0% of each run, Pallas kernels for 0% -> 0%
where the time goes in v1:
time: 614 us; the launch traced here: 613 us
  waiting for transfers between devices  491 us (80%)
  blocking collectives  70.7 us (12%)
  matrix products  15.1 us (2%)
  between operations  13.6 us (2%)
  starting transfers between devices  11 us (2%)
  local copies, waits for them, and re-layouts  10.7 us (2%)
    all_to_all x1, waiting for transfers between devices, on_device(): lax.all_to_all(jnp.stack([tokens] * lax.axis_size('tensor')), 'tensor', 0...  279 us
    reduce_scatter x1, waiting for transfers between devices, on_device(): lax.psum_scatter(partial_low, 'tensor', scatter_dimension=0, tiled=True)  213 us
    all_gather x1, blocking collectives, on_device(): lax.all_gather(low_part, 'tensor', axis=0, tiled=True).astype(jnp.bfloat16)  40.5 us
    all_to_all x1, blocking collectives, on_device(): recv = lax.all_to_all(send, 'dp', 0, 0, tiled=True)  30.2 us
    dot_general x1, matrix products, on_device(): jnp.dot(row_block, q_weight, preferred_element_type=jnp.float32)  12.8 us
  transfers between devices with their start and end apart: 2, of which 2 were waited for; matrix products, arithmetic and copies ran while one was open for 0% of the time, Pallas kernels for 0%

profile of v1, /device:TPU:2, one launch (start us, length us, event | category | flops | bytes accessed | tf_op | source)
XLA Modules:
  0.0 613.4 jit_solution(8229870156523953904)
XLA Ops:
  6.5 0.0 copy-start
  6.5 0.8 copy.24
  7.3 0.1 reshape.121
  7.4 0.0 copy-done.1
  7.4 0.0 copy-start.3
  7.5 0.0 copy-start.4
  7.5 1.2 gather_fusion
  8.7 0.1 reshape.120
  8.8 0.1 add_select_fusion.1
  9.0 0.0 copy-done.3
  9.0 0.1 pad_maximum_fusion
  9.1 0.7 gather_fusion.1
  9.7 0.3 broadcast_select_fusion
  10.0 0.0 copy-start.2
  10.0 30.2 %all_to_all.10 = bf16[16,128,512]{2,1,0:T(8,128)(2,1)S(1)} all-to-all(bf16[16,128,512]{2,1,0:T(8,128)(2,1)S(1)} %broadcast_select_fusion), channel_id=1, replica_groups=mesh['dp'=16,'tensor'=16] {'dp'}, dimensions={0} | all-to-all | bytes 4194304 | tf_op jit(solution)/shard_map/all_to_all | solution.py:31
  40.2 6.0 stack.2
  46.3 11.0 %all-to-all-start = ((bf16[16,48,8192]{2,1,0:T(8,128)(2,1)}), bf16[16,48,8192]{2,1,0:T(8,128)(2,1)}, u32[]{:S(2)}, u32[]{:S(2)}) async-start(bf16[16,48,8192]{2,1,0:T(8,128)(2,1)} %stack.2), calls=%async_computation | async-start | bytes 25165824 | tf_op jit(solution)/shard_map/all_to_all | solution.py:38
  57.2 0.0 reduce-scatter.4.cloned.1.call-start
  57.3 0.2 dynamic-slice_reduce_fusion
  57.5 0.2 reduce-window.8
  57.7 0.1 convert_reduce_fusion
  57.8 0.6 gather_fusion.2
  58.4 0.2 broadcast_select_fusion.1
  58.6 278.6 %all-to-all-done = bf16[16,48,8192]{2,1,0:T(8,128)(2,1)} async-done(((bf16[16,48,8192]{2,1,0:T(8,128)(2,1)}), bf16[16,48,8192]{2,1,0:T(8,128)(2,1)}, u32[]{:S(2)}, u32[]{:S(2)}) %all-to-all-start) | async-done | bytes 12582944 | tf_op jit(solution)/shard_map/all_to_all | solution.py:38
  337.2 1.8 select_reduce_fusion
  339.0 0.9 copy.29
  339.9 0.0 reduce-scatter.4.cloned.1.call-update
  339.9 212.6 %reduce-scatter.4.cloned.1.call-done = f32[48,64]{1,0:T(8,128)} async-done(((f32[768,64]{1,0:T(8,128)}), f32[48,64]{1,0:T(8,128)}) %reduce-scatter.4.cloned.1.call-update) | async-done | bytes 12304 | tf_op jit(solution)/shard_map/reduce_scatter | solution.py:52
  552.5 40.5 %all_gather.3 = f32[768,64]{1,0:T(8,128)S(1)} all-gather(f32[48,64]{1,0:T(8,128)} %reduce-scatter.4.cloned.1.call-done), channel_id=1, replica_groups=mesh['dp'=16,'tensor'=16] {'tensor'}, dimensions={0}, use_global_device_ids=true | all-gather | bytes 208896 | tf_op jit(solution)/shard_map/all_gather | solution.py:53
  593.0 0.1 copy.28
  593.1 0.6 fusion.3
  593.8 12.8 %fusion.1 = bf16[768,512]{1,0:T(8,128)(2,1)} fusion(f32[768,512,1]{1,0,2:T(8,128)S(1)} %fusion.3, bf16[768,8192]{1,0:T(8,128)(2,1)} %bitcast, bf16[8192,512]{1,0:T(8,128)(2,1)} %param.8), kind=kOutput, calls=%fused_computation.6 | convolution fusion | flops 6443630592 | bytes 23330816 | tf_op jit(solution)/shard_map/dot_general | solution.py:40
  (14 shorter events, 0.1 us)
Async XLA Ops:
  6.5 50.7 %copy-start = (s32[16,8]{0,1:T(8,128)S(1)}, s32[16,8]{0,1:T(8,128)}, u32[]{:S(2)}) copy-start(s32[16,8]{0,1:T(8,128)} %param.11) | copy-start | bytes 1540
  6.5 0.9 copy-start.1
  7.4 1.5 copy-start.3
  7.5 1.5 copy-start.4
  10.0 30.2 %copy-start.2 = (bf16[48,8192]{1,0:T(8,128)(2,1)S(1)}, bf16[48,8192]{1,0:T(8,128)(2,1)}, u32[]{:S(2)}) copy-start(bf16[48,8192]{1,0:T(8,128)(2,1)} %param.7) | copy-start | bytes 2359300
  46.3 291.0 %all-to-all-start = ((bf16[16,48,8192]{2,1,0:T(8,128)(2,1)}), bf16[16,48,8192]{2,1,0:T(8,128)(2,1)}, u32[]{:S(2)}, u32[]{:S(2)}) async-start(bf16[16,48,8192]{2,1,0:T(8,128)(2,1)} %stack.2), calls=%async_computation | async-start | bytes 25165824 | tf_op jit(solution)/shard_map/all_to_all | solution.py:38
  57.2 495.3 %reduce-scatter.4.cloned.1.call-start = ((), (), s32[]{:S(2)}) async-start(), calls=%async_computation.3 | async-start | bytes 417792 | tf_op jit(solution)/shard_map/reduce_scatter | solution.py:52
Sparse Core Ops, SparseCore 0:
  340.1 212.4 reduce-scatter.3
